TPU v7x, 32 devices: a whole 2x2x4 slice. The times are simulated.
32 devices in a mesh: freq: 4 (over x, core), tile: 8 (over z, y).
Axes of the slice: x: 2, y: 2, z: 4, core: 2. Of those that a mesh axis runs over, the one named last changes fastest.
Arguments:
- travel_time: float32 [512, 8, 512], P('tile', None, 'freq'), may hold values from 0 to 4
- crossing: int32 [8, 512], P('tile'), may hold values from 0 to 63
- bins: int32 [4], P('freq'), may hold values from 8 to 71
- transmission: float32 [4, 2, 64], P('freq'), may hold values from -1 to 1
- capture: bfloat16 [4, 2, 512, 512], P('freq', None, 'tile'), may hold values from -0.01171875 to 0.01171875
Outputs:
- image: float32 [2, 8, 512], P(None, 'tile')
All inputs are finite; a program needn't handle non-finite values.
Results may differ from a plain program's by a relative error of at most 0.0033.
Values may be sent and summed in bfloat16 or wider, within the bound.
No kernel may reach another device: no remote copies, remote signals or barrier semaphores. Data moves between devices by JAX's collectives and lax.ppermute only.
A program may use at most 64 MiB of HBM per device.

v0:
```python
import math
import jax
import jax.numpy as jnp
from jax import lax
from jax.sharding import PartitionSpec as P

TWO_PI = 2.0 * math.pi


def gather_shifted(block, axis_name, size):
    pieces = [block]
    for s in range(1, size):
        pairs = [(i, (i - s) % size) for i in range(size)]
        pieces.append(lax.ppermute(block, axis_name, pairs))
    return pieces


def chain(block, axis_name, size, stride, step, direction):
    positions = size // stride
    pairs = []
    for z in range(positions):
        target = z + direction
        if 0 <= target < positions and 0 <= z - direction * (step - 1) < positions:
            pairs += [(z * stride + y, target * stride + y) for y in range(stride)]
    return lax.ppermute(block, axis_name, pairs)


def line_gather(block, axis_name, size):
    positions = size // 2
    z = lax.axis_index(axis_name) // 2
    left = [block]
    right = [block]
    for j in range(1, positions):
        left.append(chain(left[-1], axis_name, size, 2, j, 1))
        right.append(chain(right[-1], axis_name, size, 2, j, -1))
    slots = left[:0:-1] + [block] + right[1:]
    return (slots, z)


def pair_swap(slots, axis_name, size):
    positions = size // 2
    centre = positions - 1
    out = []
    for i, piece in enumerate(slots):
        d = i - centre
        pairs = [
            (p * 2 + y, p * 2 + 1 - y)
            for p in range(positions)
            if 0 <= p + d < positions
            for y in range(2)
        ]
        out.append(lax.ppermute(piece, axis_name, pairs))
    return out


def gather_rows(block, axis_name, size):
    positions = size // 2
    slots, z = line_gather(block, axis_name, size)
    other = pair_swap(slots, axis_name, size)
    mine = lax.dynamic_slice_in_dim(jnp.stack(slots), positions - 1 - z, positions, 0)
    theirs = lax.dynamic_slice_in_dim(jnp.stack(other), positions - 1 - z, positions, 0)
    both = jnp.stack([mine, theirs], axis=1)
    both = jnp.roll(both, lax.axis_index(axis_name) % 2, axis=1)
    return both.reshape((size,) + block.shape)


def gather_columns(block, axis_name, size):
    outer = size // 2
    same_core = [block]
    for s in range(1, outer):
        pairs = [(i, (i - 2 * s) % size) for i in range(size)]
        same_core.append(lax.ppermute(block, axis_name, pairs))
    swap = [(i, i ^ 1) for i in range(size)]
    partner = [lax.ppermute(piece, axis_name, swap) for piece in same_core]
    return jnp.stack([jnp.stack(same_core), jnp.stack(partner)], axis=1)


def all_sum(value, axis_name, size):
    step = 1
    while step < size:
        pairs = [(i, i ^ step) for i in range(size)]
        value = value + lax.ppermute(value, axis_name, pairs)
        step *= 2
    return value


def body(travel_time, crossing, bins, transmission, capture):
    tiles = lax.axis_size("tile")
    freqs = lax.axis_size("freq")
    k = lax.axis_index("tile")
    f = lax.axis_index("freq")
    cap_all = gather_rows(capture[0], "tile", tiles)
    cap_all = jnp.moveaxis(cap_all, 0, 1)
    cap_real = cap_all[0].reshape(-1, cap_all.shape[-1])
    cap_imag = cap_all[1].reshape(-1, cap_all.shape[-1])
    rows = cap_real.shape[0]
    regrouped = lax.all_to_all(travel_time, "tile", split_axis=1, concat_axis=0, tiled=True)
    view = gather_columns(regrouped, "freq", freqs)
    view = jnp.moveaxis(view.reshape((freqs,) + regrouped.shape), 0, 2)
    elements, row_count, _, width = view.shape
    voxels = row_count * freqs * width
    scaled = TWO_PI * bins[0].astype(jnp.float32)
    angle = scaled * view.reshape(elements, voxels)
    field_real = jnp.cos(angle).astype(jnp.bfloat16)
    field_imag = (-jnp.sin(angle)).astype(jnp.bfloat16)
    stacked = jnp.concatenate([field_real, field_imag], axis=0)
    block = jnp.concatenate(
        [
            jnp.concatenate([cap_real, -cap_imag], axis=1),
            jnp.concatenate([cap_imag, cap_real], axis=1),
        ],
        axis=0,
    )
    product = jnp.dot(block, stacked, preferred_element_type=jnp.float32)
    w_real = product[:rows]
    w_imag = product[rows:]
    g_real = field_real.astype(jnp.float32)
    g_imag = field_imag.astype(jnp.float32)
    focus_real = jnp.sum(g_real * w_real - g_imag * w_imag, axis=0)
    focus_imag = jnp.sum(g_real * w_imag + g_imag * w_real, axis=0)
    outer = freqs // 2
    focus = jnp.stack([focus_real, focus_imag]).reshape(2, row_count, outer, 2, width)
    focus = jnp.roll(focus, f % 2, axis=3)
    focus = jnp.roll(focus, f // 2, axis=2).reshape(2, row_count, freqs * width)
    focus_real = focus[0]
    focus_imag = focus[1]
    cells = transmission.shape[2]
    match = crossing[None] == lax.broadcasted_iota(jnp.int32, (cells, 1, 1), 0)
    coeff_real = jnp.sum(
        jnp.where(match, transmission[0, 0][:, None, None], jnp.float32(0.0)), axis=0
    )
    coeff_imag = jnp.sum(
        jnp.where(match, transmission[0, 1][:, None, None], jnp.float32(0.0)), axis=0
    )
    square_real = coeff_real * coeff_real - coeff_imag * coeff_imag
    square_imag = 2.0 * coeff_real * coeff_imag
    part_real = square_real * focus_real - square_imag * focus_imag
    part_imag = square_real * focus_imag + square_imag * focus_real
    partial_image = jnp.stack([part_real, part_imag])
    return all_sum(partial_image, "freq", freqs)


def solution(mesh):
    in_specs = (
        P("tile", None, "freq"),
        P("tile", None),
        P("freq"),
        P("freq", None, None),
        P("freq", None, "tile", None),
    )
    out_specs = P(None, "tile", None)
    return jax.shard_map(body, mesh=mesh, in_specs=in_specs, out_specs=out_specs, check_vma=False)
```

profile of v0, /device:TPU:0, one launch (start us, length us, event | category | flops | bytes accessed | tf_op | source)
XLA Modules:
  0.0 63.5 jit_solution(8108796120977732849)
XLA Ops:
  0.0 5.1 %collective-permute-start.3 = (bf16[2,64,512]{2,1,0:T(8,128)(2,1)}, bf16[2,64,512]{2,1,0:T(8,128)(2,1)S(1)}, u32[]{:S(2)}, u32[]{:S(2)}) collective-permute-start(bf16[2,64,512]{2,1,0:T(8,128)(2,1)} %bitcast.102), channel_id=1, source_target_pairs={{0,2},{1,3},{2,4},{3,5},{4,6},{5,7},{8,10},{9,11},{10,12},{11,13},... | collective-permute-start | bytes 393224 | tf_op jit(solution)/shard_map/ppermute | solution.py:25
  5.1 1.6 %collective-permute-start.12 = (bf16[2,64,512]{2,1,0:T(8,128)(2,1)}, bf16[2,64,512]{2,1,0:T(8,128)(2,1)S(1)}, u32[]{:S(2)}, u32[]{:S(2)}) collective-permute-start(bf16[2,64,512]{2,1,0:T(8,128)(2,1)} %bitcast.103), channel_id=1, source_target_pairs={{0,1},{1,0},{2,3},{3,2},{4,5},{5,4},{6,7},{7,6},{8,9},{9,8},{10,11... | collective-permute-start | bytes 393224 | tf_op jit(solution)/shard_map/ppermute | solution.py:52
  6.7 1.3 %collective-permute-start.6 = (bf16[2,64,512]{2,1,0:T(8,128)(2,1)}, bf16[2,64,512]{2,1,0:T(8,128)(2,1)S(1)}, u32[]{:S(2)}, u32[]{:S(2)}) collective-permute-start(bf16[2,64,512]{2,1,0:T(8,128)(2,1)} %bitcast.104), channel_id=1, source_target_pairs={{2,0},{3,1},{4,2},{5,3},{6,4},{7,5},{10,8},{11,9},{12,10},{13,11},... | collective-permute-start | bytes 393224 | tf_op jit(solution)/shard_map/ppermute | solution.py:25
  7.9 1.7 %copy.14 = f32[64,8,128]{2,0,1:T(8,128)} copy(f32[64,8,128]{2,1,0:T(8,128)} %param.5) | data formatting | bytes 524288 | tf_op args[0]
  9.6 5.9 %all-to-all-start = ((f32[64,8,128]{2,0,1:T(8,128)}), f32[64,8,128]{2,0,1:T(8,128)S(1)}, u32[]{:S(2)}, u32[]{:S(2)}) async-start(f32[64,8,128]{2,0,1:T(8,128)} %copy.14), calls=%async_computation | async-start | bytes 524288 | tf_op jit(solution)/shard_map/all_to_all | solution.py:97
  15.6 0.7 %collective-permute-start.4 = (bf16[2,64,512]{2,1,0:T(8,128)(2,1)S(1)}, bf16[2,64,512]{2,1,0:T(8,128)(2,1)S(1)}, u32[]{:S(2)}, u32[]{:S(2)}) collective-permute-start(bf16[2,64,512]{2,1,0:T(8,128)(2,1)S(1)} %collective-permute-done.3), channel_id=1, source_target_pairs={{2,4},{3,5},{4,6},{5,7},{10,12},{11,13},{12,14},{13,15},{18,20},{1... | collective-permute-start | bytes 393224 | tf_op jit(solution)/shard_map/ppermute | solution.py:25
  16.3 0.8 %slice_bitcast_fusion = (f32[64]{0:T(128)S(1)}, f32[64]{0:T(128)S(1)}) fusion(f32[1,2,64]{2,1,0:T(2,128)} %param.8), kind=kLoop, calls=%fused_computation.67 | loop fusion | bytes 1024 | tf_op jit(solution)/shard_map/jit(_where)/broadcast_in_dim | solution.py:133
  17.7 0.8 %select_reduce_fusion.1 = (f32[512]{0:T(512)S(1)}, f32[512]{0:T(512)S(1)}) fusion(f32[64]{0:T(128)S(1)} %get-tuple-element.20, s32[512]{0:T(512)} %bitcast.111, f32[64]{0:T(128)S(1)} %get-tuple-element.19), kind=kLoop, calls=%fused_computation.49 | loop fusion | flops 162816 | bytes 6656 | tf_op jit(solution)/shard_map/reduce_sum | solution.py:129
  18.5 1.3 %collective-permute-start.7 = (bf16[2,64,512]{2,1,0:T(8,128)(2,1)S(1)}, bf16[2,64,512]{2,1,0:T(8,128)(2,1)S(1)}, u32[]{:S(2)}, u32[]{:S(2)}) collective-permute-start(bf16[2,64,512]{2,1,0:T(8,128)(2,1)S(1)} %collective-permute-done.6), channel_id=1, source_target_pairs={{2,0},{3,1},{4,2},{5,3},{10,8},{11,9},{12,10},{13,11},{18,16},{19,... | collective-permute-start | bytes 393224 | tf_op jit(solution)/shard_map/ppermute | solution.py:25
  19.8 0.7 %collective-permute-start.5 = (bf16[2,64,512]{2,1,0:T(8,128)(2,1)S(1)}, bf16[2,64,512]{2,1,0:T(8,128)(2,1)S(1)}, u32[]{:S(2)}, u32[]{:S(2)}) collective-permute-start(bf16[2,64,512]{2,1,0:T(8,128)(2,1)S(1)} %collective-permute-done.4), channel_id=1, source_target_pairs={{4,6},{5,7},{12,14},{13,15},{20,22},{21,23},{28,30},{29,31}} | collective-permute-start | bytes 393224 | tf_op jit(solution)/shard_map/ppermute | solution.py:25
  20.5 0.7 %collective-permute-start.11 = (bf16[2,64,512]{2,1,0:T(8,128)(2,1)S(1)}, bf16[2,64,512]{2,1,0:T(8,128)(2,1)S(1)}, u32[]{:S(2)}, u32[]{:S(2)}) collective-permute-start(bf16[2,64,512]{2,1,0:T(8,128)(2,1)S(1)} %collective-permute-done.3), channel_id=1, source_target_pairs={{2,3},{3,2},{4,5},{5,4},{6,7},{7,6},{10,11},{11,10},{12,13},{13,12... | collective-permute-start | bytes 393224 | tf_op jit(solution)/shard_map/ppermute | solution.py:52
  21.2 3.9 %collective-permute-start.13 = (bf16[2,64,512]{2,1,0:T(8,128)(2,1)S(1)}, bf16[2,64,512]{2,1,0:T(8,128)(2,1)S(1)}, u32[]{:S(2)}, u32[]{:S(2)}) collective-permute-start(bf16[2,64,512]{2,1,0:T(8,128)(2,1)S(1)} %collective-permute-done.6), channel_id=1, source_target_pairs={{0,1},{1,0},{2,3},{3,2},{4,5},{5,4},{8,9},{9,8},{10,11},{11,10},{1... | collective-permute-start | bytes 393224 | tf_op jit(solution)/shard_map/ppermute | solution.py:52
  25.1 3.0 %collective-permute-done.7 = bf16[2,64,512]{2,1,0:T(8,128)(2,1)S(1)} collective-permute-done((bf16[2,64,512]{2,1,0:T(8,128)(2,1)S(1)}, bf16[2,64,512]{2,1,0:T(8,128)(2,1)S(1)}, u32[]{:S(2)}, u32[]{:S(2)}) %collective-permute-start.7) | collective-permute-done | bytes 131104 | tf_op jit(solution)/shard_map/ppermute | solution.py:25
  28.1 0.7 %collective-permute-start.10 = (bf16[2,64,512]{2,1,0:T(8,128)(2,1)S(1)}, bf16[2,64,512]{2,1,0:T(8,128)(2,1)S(1)}, u32[]{:S(2)}, u32[]{:S(2)}) collective-permute-start(bf16[2,64,512]{2,1,0:T(8,128)(2,1)S(1)} %collective-permute-done.4), channel_id=1, source_target_pairs={{4,5},{5,4},{6,7},{7,6},{12,13},{13,12},{14,15},{15,14},{20,21},{2... | collective-permute-start | bytes 393224 | tf_op jit(solution)/shard_map/ppermute | solution.py:52
  28.7 1.3 %collective-permute-start.8 = (bf16[2,64,512]{2,1,0:T(8,128)(2,1)S(1)}, bf16[2,64,512]{2,1,0:T(8,128)(2,1)S(1)}, u32[]{:S(2)}, u32[]{:S(2)}) collective-permute-start(bf16[2,64,512]{2,1,0:T(8,128)(2,1)S(1)} %collective-permute-done.7), channel_id=1, source_target_pairs={{2,0},{3,1},{10,8},{11,9},{18,16},{19,17},{26,24},{27,25}} | collective-permute-start | bytes 393224 | tf_op jit(solution)/shard_map/ppermute | solution.py:25
  30.2 6.5 %collective-permute-done.8 = bf16[2,64,512]{2,1,0:T(8,128)(2,1)S(1)} collective-permute-done((bf16[2,64,512]{2,1,0:T(8,128)(2,1)S(1)}, bf16[2,64,512]{2,1,0:T(8,128)(2,1)S(1)}, u32[]{:S(2)}, u32[]{:S(2)}) %collective-permute-start.8) | collective-permute-done | bytes 131104 | tf_op jit(solution)/shard_map/ppermute | solution.py:25
  36.6 0.7 %collective-permute-start.9 = (bf16[2,64,512]{2,1,0:T(8,128)(2,1)S(1)}, bf16[2,64,512]{2,1,0:T(8,128)(2,1)S(1)}, u32[]{:S(2)}, u32[]{:S(2)}) collective-permute-start(bf16[2,64,512]{2,1,0:T(8,128)(2,1)S(1)} %collective-permute-done.5), channel_id=1, source_target_pairs={{6,7},{7,6},{14,15},{15,14},{22,23},{23,22},{30,31},{31,30}} | collective-permute-start | bytes 393224 | tf_op jit(solution)/shard_map/ppermute | solution.py:52
  37.4 3.4 %collective-permute-start.14 = (bf16[2,64,512]{2,1,0:T(8,128)(2,1)S(1)}, bf16[2,64,512]{2,1,0:T(8,128)(2,1)S(1)}, u32[]{:S(2)}, u32[]{:S(2)}) collective-permute-start(bf16[2,64,512]{2,1,0:T(8,128)(2,1)S(1)} %collective-permute-done.7), channel_id=1, source_target_pairs={{0,1},{1,0},{2,3},{3,2},{8,9},{9,8},{10,11},{11,10},{16,17},{17,16... | collective-permute-start | bytes 393224 | tf_op jit(solution)/shard_map/ppermute | solution.py:52
  40.8 2.5 %collective-permute-start.15 = (bf16[2,64,512]{2,1,0:T(8,128)(2,1)S(1)}, bf16[2,64,512]{2,1,0:T(8,128)(2,1)S(1)}, u32[]{:S(2)}, u32[]{:S(2)}) collective-permute-start(bf16[2,64,512]{2,1,0:T(8,128)(2,1)S(1)} %collective-permute-done.8), channel_id=1, source_target_pairs={{0,1},{1,0},{8,9},{9,8},{16,17},{17,16},{24,25},{25,24}} | collective-permute-start | bytes 393224 | tf_op jit(solution)/shard_map/ppermute | solution.py:52
  43.3 1.6 %collective-permute-start = (f32[512,1,128]{2,0,1:T(8,128)S(1)}, f32[512,1,128]{2,0,1:T(8,128)S(1)}, u32[]{:S(2)}, u32[]{:S(2)}) collective-permute-start(f32[512,1,128]{2,0,1:T(8,128)S(1)} %bitcast.95), channel_id=1, source_target_pairs={{0,16},{8,24},{16,0},{24,8},{1,17},{9,25},{17,1},{25,9},{2,18},{10... | collective-permute-start | bytes 786440 | tf_op jit(solution)/shard_map/ppermute | solution.py:72
  45.0 0.5 collective-permute-done.14
  45.5 2.2 %collective-permute-done.15 = bf16[2,64,512]{2,1,0:T(8,128)(2,1)S(1)} collective-permute-done((bf16[2,64,512]{2,1,0:T(8,128)(2,1)S(1)}, bf16[2,64,512]{2,1,0:T(8,128)(2,1)S(1)}, u32[]{:S(2)}, u32[]{:S(2)}) %collective-permute-start.15) | collective-permute-done | bytes 131104 | tf_op jit(solution)/shard_map/ppermute | solution.py:52
  47.7 0.7 %fusion.14 = bf16[4,2,2,64,512]{4,3,2,1,0:T(8,128)(2,1)S(1)} fusion(s32[]{:T(128)S(6)} %select_n.83, bf16[4,1,2,64,512]{4,3,2,1,0:T(8,128)(2,1)S(1)} %dynamic-slice_bitcast_fusion.1, bf16[4,1,2,64,512]{4,3,2,1,0:T(8,128)(2,1)S(1)} %dynamic-slice_bitcast_fusion), kind=kLoop, calls=%fused_computation.22 | loop fusion | flops 1572864 | bytes 2097156 | tf_op jit(solution)/shard_map/jit(_roll_dynamic)/concatenate | solution.py:63
  48.5 1.2 %collective-permute-done = f32[512,1,128]{2,0,1:T(8,128)S(1)} collective-permute-done((f32[512,1,128]{2,0,1:T(8,128)S(1)}, f32[512,1,128]{2,0,1:T(8,128)S(1)}, u32[]{:S(2)}, u32[]{:S(2)}) %collective-permute-start) | collective-permute-done | bytes 262176 | tf_op jit(solution)/shard_map/ppermute | solution.py:72
  49.9 1.4 %collective-permute-done.2 = f32[512,1,128]{2,0,1:T(8,128)S(1)} collective-permute-done((f32[512,1,128]{2,0,1:T(8,128)S(1)}, f32[512,1,128]{2,0,1:T(8,128)S(1)}, u32[]{:S(2)}, u32[]{:S(2)}) %collective-permute-start.2) | collective-permute-done | bytes 262176 | tf_op jit(solution)/shard_map/ppermute | solution.py:74
  51.3 3.8 %cosine_convert_fusion = (bf16[2,2,512,1,128]{4,2,0,3,1:T(8,128)(2,1)S(1)}, bf16[2,2,512,1,128]{4,2,0,3,1:T(8,128)(2,1)S(1)}) fusion(f32[2,1,512,1,128]{4,2,0,3,1:T(8,128)S(1)} %maximum_bitcast_fusion.1, f32[2,1,512,1,128]{4,2,0,3,1:T(8,128)S(1)} %maximum_bitcast_fusion, f32[]{:T(128)} %bitcast.4), kind=kLoop, calls=%fused_computation.28 | loop fusion | flops 1310720 | bytes 2097156 | tf_op jit(solution)/shard_map/convert.1
  56.2 1.2 %fusion = f32[1024,512]{1,0:T(8,128)S(1)} fusion(bf16[512,512]{1,0:T(8,128)(2,1)S(1)} %bitcast.98, bf16[512,512]{1,0:T(8,128)(2,1)S(1)} %bitcast.94, bf16[512,512]{1,0:T(8,128)(2,1)S(1)} %bitcast_negate_fusion, bf16[512,512]{1,0:T(8,128)(2,1)S(1)} %get-tuple-element.21, bf16[512,512]{1,0:T(8,128)(2,1)S(1)} %get-tuple-element.22), kind=kOutput, calls=%fused_computation.4 | convolution fusion | flops 1084227584 | bytes 4718592 | tf_op jit(solution)/shard_map/dot_general | solution.py:114
  57.5 0.4 fusion.11
  58.2 1.0 %collective-permute-done.16 = f32[2,1,512]{2,1,0:T(1,128)S(1)} collective-permute-done((f32[2,1,512]{2,1,0:T(1,128)S(1)}, f32[2,1,512]{2,1,0:T(1,128)S(1)}, u32[]{:S(2)}, u32[]{:S(2)}) %collective-permute-start.16) | collective-permute-done | bytes 4128 | tf_op jit(solution)/shard_map/ppermute | solution.py:82
  59.2 1.5 %collective-permute-start.17 = (f32[2,1,512]{2,1,0:T(1,128)S(1)}, f32[2,1,512]{2,1,0:T(1,128)S(1)}, u32[]{:S(2)}, u32[]{:S(2)}) collective-permute-start(f32[2,1,512]{2,1,0:T(1,128)S(1)} %fusion.23), channel_id=1, source_target_pairs={{0,16},{8,24},{16,0},{24,8},{1,17},{9,25},{17,1},{25,9},{2,18},{10... | collective-permute-start | bytes 12296 | tf_op jit(solution)/shard_map/ppermute | solution.py:82
  60.8 2.1 %collective-permute-done.17 = f32[2,1,512]{2,1,0:T(1,128)S(1)} collective-permute-done((f32[2,1,512]{2,1,0:T(1,128)S(1)}, f32[2,1,512]{2,1,0:T(1,128)S(1)}, u32[]{:S(2)}, u32[]{:S(2)}) %collective-permute-start.17) | collective-permute-done | bytes 4128 | tf_op jit(solution)/shard_map/ppermute | solution.py:82
  62.9 0.6 fusion.26
  (48 shorter events, 1.9 us)
Async XLA Ops:
  0.0 30.1 %copy-start = (bf16[1,2,64,512]{3,2,1,0:T(8,128)(2,1)S(1)}, bf16[1,2,64,512]{3,2,1,0:T(8,128)(2,1)}, u32[]{:S(2)}) copy-start(bf16[1,2,64,512]{3,2,1,0:T(8,128)(2,1)} %param.9) | copy-start | bytes 393220
  0.0 15.6 %collective-permute-start.3 = (bf16[2,64,512]{2,1,0:T(8,128)(2,1)}, bf16[2,64,512]{2,1,0:T(8,128)(2,1)S(1)}, u32[]{:S(2)}, u32[]{:S(2)}) collective-permute-start(bf16[2,64,512]{2,1,0:T(8,128)(2,1)} %bitcast.102), channel_id=1, source_target_pairs={{0,2},{1,3},{2,4},{3,5},{4,6},{5,7},{8,10},{9,11},{10,12},{11,13},... | collective-permute-start | bytes 393224 | tf_op jit(solution)/shard_map/ppermute | solution.py:25
  5.1 39.8 %collective-permute-start.12 = (bf16[2,64,512]{2,1,0:T(8,128)(2,1)}, bf16[2,64,512]{2,1,0:T(8,128)(2,1)S(1)}, u32[]{:S(2)}, u32[]{:S(2)}) collective-permute-start(bf16[2,64,512]{2,1,0:T(8,128)(2,1)} %bitcast.103), channel_id=1, source_target_pairs={{0,1},{1,0},{2,3},{3,2},{4,5},{5,4},{6,7},{7,6},{8,9},{9,8},{10,11... | collective-permute-start | bytes 393224 | tf_op jit(solution)/shard_map/ppermute | solution.py:52
  6.7 11.8 %collective-permute-start.6 = (bf16[2,64,512]{2,1,0:T(8,128)(2,1)}, bf16[2,64,512]{2,1,0:T(8,128)(2,1)S(1)}, u32[]{:S(2)}, u32[]{:S(2)}) collective-permute-start(bf16[2,64,512]{2,1,0:T(8,128)(2,1)} %bitcast.104), channel_id=1, source_target_pairs={{2,0},{3,1},{4,2},{5,3},{6,4},{7,5},{10,8},{11,9},{12,10},{13,11},... | collective-permute-start | bytes 393224 | tf_op jit(solution)/shard_map/ppermute | solution.py:25
  9.6 33.6 %all-to-all-start = ((f32[64,8,128]{2,0,1:T(8,128)}), f32[64,8,128]{2,0,1:T(8,128)S(1)}, u32[]{:S(2)}, u32[]{:S(2)}) async-start(f32[64,8,128]{2,0,1:T(8,128)} %copy.14), calls=%async_computation | async-start | bytes 524288 | tf_op jit(solution)/shard_map/all_to_all | solution.py:97
  15.6 4.2 %collective-permute-start.4 = (bf16[2,64,512]{2,1,0:T(8,128)(2,1)S(1)}, bf16[2,64,512]{2,1,0:T(8,128)(2,1)S(1)}, u32[]{:S(2)}, u32[]{:S(2)}) collective-permute-start(bf16[2,64,512]{2,1,0:T(8,128)(2,1)S(1)} %collective-permute-done.3), channel_id=1, source_target_pairs={{2,4},{3,5},{4,6},{5,7},{10,12},{11,13},{12,14},{13,15},{18,20},{1... | collective-permute-start | bytes 393224 | tf_op jit(solution)/shard_map/ppermute | solution.py:25
  18.5 9.6 %collective-permute-start.7 = (bf16[2,64,512]{2,1,0:T(8,128)(2,1)S(1)}, bf16[2,64,512]{2,1,0:T(8,128)(2,1)S(1)}, u32[]{:S(2)}, u32[]{:S(2)}) collective-permute-start(bf16[2,64,512]{2,1,0:T(8,128)(2,1)S(1)} %collective-permute-done.6), channel_id=1, source_target_pairs={{2,0},{3,1},{4,2},{5,3},{10,8},{11,9},{12,10},{13,11},{18,16},{19,... | collective-permute-start | bytes 393224 | tf_op jit(solution)/shard_map/ppermute | solution.py:25
  19.8 8.9 %collective-permute-start.5 = (bf16[2,64,512]{2,1,0:T(8,128)(2,1)S(1)}, bf16[2,64,512]{2,1,0:T(8,128)(2,1)S(1)}, u32[]{:S(2)}, u32[]{:S(2)}) collective-permute-start(bf16[2,64,512]{2,1,0:T(8,128)(2,1)S(1)} %collective-permute-done.4), channel_id=1, source_target_pairs={{4,6},{5,7},{12,14},{13,15},{20,22},{21,23},{28,30},{29,31}} | collective-permute-start | bytes 393224 | tf_op jit(solution)/shard_map/ppermute | solution.py:25
  20.5 22.8 %collective-permute-start.11 = (bf16[2,64,512]{2,1,0:T(8,128)(2,1)S(1)}, bf16[2,64,512]{2,1,0:T(8,128)(2,1)S(1)}, u32[]{:S(2)}, u32[]{:S(2)}) collective-permute-start(bf16[2,64,512]{2,1,0:T(8,128)(2,1)S(1)} %collective-permute-done.3), channel_id=1, source_target_pairs={{2,3},{3,2},{4,5},{5,4},{6,7},{7,6},{10,11},{11,10},{12,13},{13,12... | collective-permute-start | bytes 393224 | tf_op jit(solution)/shard_map/ppermute | solution.py:52
  21.2 23.8 %collective-permute-start.13 = (bf16[2,64,512]{2,1,0:T(8,128)(2,1)S(1)}, bf16[2,64,512]{2,1,0:T(8,128)(2,1)S(1)}, u32[]{:S(2)}, u32[]{:S(2)}) collective-permute-start(bf16[2,64,512]{2,1,0:T(8,128)(2,1)S(1)} %collective-permute-done.6), channel_id=1, source_target_pairs={{0,1},{1,0},{2,3},{3,2},{4,5},{5,4},{8,9},{9,8},{10,11},{11,10},{1... | collective-permute-start | bytes 393224 | tf_op jit(solution)/shard_map/ppermute | solution.py:52
  28.1 12.7 %collective-permute-start.10 = (bf16[2,64,512]{2,1,0:T(8,128)(2,1)S(1)}, bf16[2,64,512]{2,1,0:T(8,128)(2,1)S(1)}, u32[]{:S(2)}, u32[]{:S(2)}) collective-permute-start(bf16[2,64,512]{2,1,0:T(8,128)(2,1)S(1)} %collective-permute-done.4), channel_id=1, source_target_pairs={{4,5},{5,4},{6,7},{7,6},{12,13},{13,12},{14,15},{15,14},{20,21},{2... | collective-permute-start | bytes 393224 | tf_op jit(solution)/shard_map/ppermute | solution.py:52
  28.7 7.9 %collective-permute-start.8 = (bf16[2,64,512]{2,1,0:T(8,128)(2,1)S(1)}, bf16[2,64,512]{2,1,0:T(8,128)(2,1)S(1)}, u32[]{:S(2)}, u32[]{:S(2)}) collective-permute-start(bf16[2,64,512]{2,1,0:T(8,128)(2,1)S(1)} %collective-permute-done.7), channel_id=1, source_target_pairs={{2,0},{3,1},{10,8},{11,9},{18,16},{19,17},{26,24},{27,25}} | collective-permute-start | bytes 393224 | tf_op jit(solution)/shard_map/ppermute | solution.py:25
  36.6 0.7 %collective-permute-start.9 = (bf16[2,64,512]{2,1,0:T(8,128)(2,1)S(1)}, bf16[2,64,512]{2,1,0:T(8,128)(2,1)S(1)}, u32[]{:S(2)}, u32[]{:S(2)}) collective-permute-start(bf16[2,64,512]{2,1,0:T(8,128)(2,1)S(1)} %collective-permute-done.5), channel_id=1, source_target_pairs={{6,7},{7,6},{14,15},{15,14},{22,23},{23,22},{30,31},{31,30}} | collective-permute-start | bytes 393224 | tf_op jit(solution)/shard_map/ppermute | solution.py:52
  37.4 8.1 %collective-permute-start.14 = (bf16[2,64,512]{2,1,0:T(8,128)(2,1)S(1)}, bf16[2,64,512]{2,1,0:T(8,128)(2,1)S(1)}, u32[]{:S(2)}, u32[]{:S(2)}) collective-permute-start(bf16[2,64,512]{2,1,0:T(8,128)(2,1)S(1)} %collective-permute-done.7), channel_id=1, source_target_pairs={{0,1},{1,0},{2,3},{3,2},{8,9},{9,8},{10,11},{11,10},{16,17},{17,16... | collective-permute-start | bytes 393224 | tf_op jit(solution)/shard_map/ppermute | solution.py:52
  40.8 6.9 %collective-permute-start.15 = (bf16[2,64,512]{2,1,0:T(8,128)(2,1)S(1)}, bf16[2,64,512]{2,1,0:T(8,128)(2,1)S(1)}, u32[]{:S(2)}, u32[]{:S(2)}) collective-permute-start(bf16[2,64,512]{2,1,0:T(8,128)(2,1)S(1)} %collective-permute-done.8), channel_id=1, source_target_pairs={{0,1},{1,0},{8,9},{9,8},{16,17},{17,16},{24,25},{25,24}} | collective-permute-start | bytes 393224 | tf_op jit(solution)/shard_map/ppermute | solution.py:52
  43.3 6.4 %collective-permute-start = (f32[512,1,128]{2,0,1:T(8,128)S(1)}, f32[512,1,128]{2,0,1:T(8,128)S(1)}, u32[]{:S(2)}, u32[]{:S(2)}) collective-permute-start(f32[512,1,128]{2,0,1:T(8,128)S(1)} %bitcast.95), channel_id=1, source_target_pairs={{0,16},{8,24},{16,0},{24,8},{1,17},{9,25},{17,1},{25,9},{2,18},{10... | collective-permute-start | bytes 786440 | tf_op jit(solution)/shard_map/ppermute | solution.py:72
  44.9 5.0 %collective-permute-start.1 = (f32[512,1,128]{2,0,1:T(8,128)S(1)}, f32[512,1,128]{2,0,1:T(8,128)S(1)}, u32[]{:S(2)}, u32[]{:S(2)}) collective-permute-start(f32[512,1,128]{2,0,1:T(8,128)S(1)} %bitcast.96), channel_id=1, source_target_pairs={{0,8},{8,0},{16,24},{24,16},{1,9},{9,1},{17,25},{25,17},{2,10},{10... | collective-permute-start | bytes 786440 | tf_op jit(solution)/shard_map/ppermute | solution.py:74
  49.7 1.5 %collective-permute-start.2 = (f32[512,1,128]{2,0,1:T(8,128)S(1)}, f32[512,1,128]{2,0,1:T(8,128)S(1)}, u32[]{:S(2)}, u32[]{:S(2)}) collective-permute-start(f32[512,1,128]{2,0,1:T(8,128)S(1)} %collective-permute-done), channel_id=1, source_target_pairs={{0,8},{8,0},{16,24},{24,16},{1,9},{9,1},{17,25},{25,17},{2,10},{10... | collective-permute-start | bytes 786440 | tf_op jit(solution)/shard_map/ppermute | solution.py:74
  58.0 1.2 %collective-permute-start.16 = (f32[2,1,512]{2,1,0:T(1,128)S(1)}, f32[2,1,512]{2,1,0:T(1,128)S(1)}, u32[]{:S(2)}, u32[]{:S(2)}) collective-permute-start(f32[2,1,512]{2,1,0:T(1,128)S(1)} %pad_maximum_fusion), channel_id=1, source_target_pairs={{0,8},{8,0},{16,24},{24,16},{1,9},{9,1},{17,25},{25,17},{2,10},{10... | collective-permute-start | bytes 12296 | tf_op jit(solution)/shard_map/ppermute | solution.py:82
  59.2 3.7 %collective-permute-start.17 = (f32[2,1,512]{2,1,0:T(1,128)S(1)}, f32[2,1,512]{2,1,0:T(1,128)S(1)}, u32[]{:S(2)}, u32[]{:S(2)}) collective-permute-start(f32[2,1,512]{2,1,0:T(1,128)S(1)} %fusion.23), channel_id=1, source_target_pairs={{0,16},{8,24},{16,0},{24,8},{1,17},{9,25},{17,1},{25,9},{2,18},{10... | collective-permute-start | bytes 12296 | tf_op jit(solution)/shard_map/ppermute | solution.py:82
where the time goes:
time: 64 us; the launch traced here: 63.5 us
  starting transfers between devices  32.9 us (51%)
  waiting for transfers between devices  17.9 us (28%)
  other arithmetic  6.57 us (10%)
  local copies, waits for them, and re-layouts  3.82 us (6%)
  matrix products  1.24 us (2%)
  between operations  1.11 us (2%)
    ppermute x7, starting transfers between devices, pair_swap(): out.append(lax.ppermute(piece, axis_name, pairs))  13.3 us
    ppermute x6, starting transfers between devices, chain(): return lax.ppermute(block, axis_name, pairs)  10.3 us
    ppermute x6, waiting for transfers between devices, chain(): return lax.ppermute(block, axis_name, pairs)  9.43 us
    all_to_all x1, starting transfers between devices, body(): lax.all_to_all(travel_time, 'tile', split_axis=1, concat_axis=0, tiled=True)  5.94 us
    another operation x1, other arithmetic  3.84 us
    ppermute x2, waiting for transfers between devices, all_sum(): value = value + lax.ppermute(value, axis_name, pairs)  3.16 us
    ppermute x7, waiting for transfers between devices, pair_swap(): out.append(lax.ppermute(piece, axis_name, pairs))  2.63 us
    unnamed x15, local copies, waits for them, and re-layouts  1.84 us
  transfers between devices with their start and end apart: 19, of which 8 were waited for; matrix products, arithmetic and copies ran while one was open for 7% of the time, Pallas kernels for 0%

commit v1 on v0

--- a/solution.py
+++ b/solution.py
@@ -94,7 +94,15 @@
     cap_real = cap_all[0].reshape(-1, cap_all.shape[-1])
     cap_imag = cap_all[1].reshape(-1, cap_all.shape[-1])
     rows = cap_real.shape[0]
-    regrouped = lax.all_to_all(travel_time, "tile", split_axis=1, concat_axis=0, tiled=True)
+    regrouped = jnp.concatenate(
+        jax.lax.all_to_all(
+            jnp.stack(jnp.split(travel_time, jax.lax.axis_size("tile"), axis=1)),
+            axis_name="tile",
+            split_axis=0,
+            concat_axis=0,
+        ),
+        axis=0,
+    )
     view = gather_columns(regrouped, "freq", freqs)
     view = jnp.moveaxis(view.reshape((freqs,) + regrouped.shape), 0, 2)
     elements, row_count, _, width = view.shape

time: 64 us -> 69.8 us (1.091)
  local copies, waits for them, and re-layouts: 3.82 us -> 9.57 us
    unnamed x15 -> x21, local copies, waits for them, and re-layouts: 1.84 us -> 4.37 us
    split x0 -> x1, local copies, waits for them, and re-layouts: none -> 2.42 us  [body(): jnp.split(travel_time, jax.lax.axis_size('tile'), axis=1)]
    another operation x2 -> x3, local copies, waits for them, and re-layouts: 0.07 us -> 1.69 us
  transfers between devices with their start and end apart: 19 -> 19, of which waited for: 8 -> 8; matrix products, arithmetic and copies ran while one was open for 7% -> 14% of each run, Pallas kernels for 0% -> 0%
where the time goes in v1:
time: 69.8 us; the launch traced here: 69.2 us
  starting transfers between devices  32.9 us (47%)
  waiting for transfers between devices  17.8 us (26%)
  local copies, waits for them, and re-layouts  9.57 us (14%)
  other arithmetic  6.57 us (9%)
  matrix products  1.24 us (2%)
  between operations  1.11 us (2%)
    ppermute x7, starting transfers between devices, pair_swap(): out.append(lax.ppermute(piece, axis_name, pairs))  13.3 us
    ppermute x6, starting transfers between devices, chain(): return lax.ppermute(block, axis_name, pairs)  10.3 us
    ppermute x6, waiting for transfers between devices, chain(): return lax.ppermute(block, axis_name, pairs)  9.43 us
    all_to_all x1, starting transfers between devices, body(): jax.lax.all_to_all(jnp.stack(jnp.split(travel_time, jax.lax.axis_size('ti...  5.94 us
    unnamed x21, local copies, waits for them, and re-layouts  4.37 us
    another operation x1, other arithmetic  3.84 us
    ppermute x2, waiting for transfers between devices, all_sum(): value = value + lax.ppermute(value, axis_name, pairs)  3.14 us
    ppermute x7, waiting for transfers between devices, pair_swap(): out.append(lax.ppermute(piece, axis_name, pairs))  2.63 us
  transfers between devices with their start and end apart: 19, of which 8 were waited for; matrix products, arithmetic and copies ran while one was open for 14% of the time, Pallas kernels for 0%

profile of v1, /device:TPU:0, one launch (start us, length us, event | category | flops | bytes accessed | tf_op | source)
XLA Modules:
  0.0 69.2 jit_solution(4904044031238596953)
XLA Ops:
  0.0 5.1 %collective-permute-start.3 = (bf16[2,64,512]{2,1,0:T(8,128)(2,1)}, bf16[2,64,512]{2,1,0:T(8,128)(2,1)S(1)}, u32[]{:S(2)}, u32[]{:S(2)}) collective-permute-start(bf16[2,64,512]{2,1,0:T(8,128)(2,1)} %bitcast.127), channel_id=1, source_target_pairs={{0,2},{1,3},{2,4},{3,5},{4,6},{5,7},{8,10},{9,11},{10,12},{11,13},... | collective-permute-start | bytes 393224 | tf_op jit(solution)/shard_map/ppermute | solution.py:25
  5.1 1.6 %collective-permute-start.12 = (bf16[2,64,512]{2,1,0:T(8,128)(2,1)}, bf16[2,64,512]{2,1,0:T(8,128)(2,1)S(1)}, u32[]{:S(2)}, u32[]{:S(2)}) collective-permute-start(bf16[2,64,512]{2,1,0:T(8,128)(2,1)} %bitcast.128), channel_id=1, source_target_pairs={{0,1},{1,0},{2,3},{3,2},{4,5},{5,4},{6,7},{7,6},{8,9},{9,8},{10,11... | collective-permute-start | bytes 393224 | tf_op jit(solution)/shard_map/ppermute | solution.py:52
  6.7 1.3 %collective-permute-start.6 = (bf16[2,64,512]{2,1,0:T(8,128)(2,1)}, bf16[2,64,512]{2,1,0:T(8,128)(2,1)S(1)}, u32[]{:S(2)}, u32[]{:S(2)}) collective-permute-start(bf16[2,64,512]{2,1,0:T(8,128)(2,1)} %bitcast.129), channel_id=1, source_target_pairs={{2,0},{3,1},{4,2},{5,3},{6,4},{7,5},{10,8},{11,9},{12,10},{13,11},... | collective-permute-start | bytes 393224 | tf_op jit(solution)/shard_map/ppermute | solution.py:25
  7.9 2.4 %fusion.25 = (f32[64,1,128]{2,1,0:T(1,128)S(1)}, f32[64,1,128]{2,1,0:T(1,128)S(1)}, f32[64,1,128]{2,1,0:T(1,128)S(1)}, f32[64,1,128]{2,1,0:T(1,128)S(1)}, f32[64...) fusion(f32[64,8,128]{2,1,0:T(8,128)} %param.5), kind=kLoop, calls=%fused_computation.81 | loop fusion | bytes 524288 | tf_op jit(solution)/shard_map/split | solution.py:99
  10.4 0.6 constant_dynamic-update-slice_fusion.7
  11.0 0.6 constant_dynamic-update-slice_fusion.6
  14.6 0.6 constant_dynamic-update-slice_fusion
  15.2 5.9 %all-to-all-start = ((f32[8,64,1,128]{3,1,2,0:T(8,128)}), f32[8,64,1,128]{3,1,2,0:T(8,128)S(1)}, u32[]{:S(2)}, u32[]{:S(2)}) async-start(f32[8,64,1,128]{3,1,2,0:T(8,128)} %constant_dynamic-update-slice_fusion), calls=%async_computation | async-start | bytes 524288 | tf_op jit(solution)/shard_map/all_to_all | solution.py:98
  21.2 0.7 collective-permute-start.4
  21.8 0.8 %slice_bitcast_fusion = (f32[64]{0:T(128)S(1)}, f32[64]{0:T(128)S(1)}) fusion(f32[1,2,64]{2,1,0:T(2,128)} %param.8), kind=kLoop, calls=%fused_computation.75 | loop fusion | bytes 1024 | tf_op jit(solution)/shard_map/jit(_where)/broadcast_in_dim | solution.py:141
  23.3 0.8 %select_reduce_fusion.1 = (f32[512]{0:T(512)S(1)}, f32[512]{0:T(512)S(1)}) fusion(f32[64]{0:T(128)S(1)} %get-tuple-element.28, s32[512]{0:T(512)} %bitcast.136, f32[64]{0:T(128)S(1)} %get-tuple-element.27), kind=kLoop, calls=%fused_computation.49 | loop fusion | flops 162816 | bytes 6656 | tf_op jit(solution)/shard_map/reduce_sum | solution.py:137
  24.1 1.3 %collective-permute-start.7 = (bf16[2,64,512]{2,1,0:T(8,128)(2,1)S(1)}, bf16[2,64,512]{2,1,0:T(8,128)(2,1)S(1)}, u32[]{:S(2)}, u32[]{:S(2)}) collective-permute-start(bf16[2,64,512]{2,1,0:T(8,128)(2,1)S(1)} %collective-permute-done.6), channel_id=1, source_target_pairs={{2,0},{3,1},{4,2},{5,3},{10,8},{11,9},{12,10},{13,11},{18,16},{19,... | collective-permute-start | bytes 393224 | tf_op jit(solution)/shard_map/ppermute | solution.py:25
  25.4 0.7 collective-permute-start.5
  26.1 0.7 collective-permute-start.11
  26.8 3.9 %collective-permute-start.13 = (bf16[2,64,512]{2,1,0:T(8,128)(2,1)S(1)}, bf16[2,64,512]{2,1,0:T(8,128)(2,1)S(1)}, u32[]{:S(2)}, u32[]{:S(2)}) collective-permute-start(bf16[2,64,512]{2,1,0:T(8,128)(2,1)S(1)} %collective-permute-done.6), channel_id=1, source_target_pairs={{0,1},{1,0},{2,3},{3,2},{4,5},{5,4},{8,9},{9,8},{10,11},{11,10},{1... | collective-permute-start | bytes 393224 | tf_op jit(solution)/shard_map/ppermute | solution.py:52
  30.7 3.0 %collective-permute-done.7 = bf16[2,64,512]{2,1,0:T(8,128)(2,1)S(1)} collective-permute-done((bf16[2,64,512]{2,1,0:T(8,128)(2,1)S(1)}, bf16[2,64,512]{2,1,0:T(8,128)(2,1)S(1)}, u32[]{:S(2)}, u32[]{:S(2)}) %collective-permute-start.7) | collective-permute-done | bytes 131104 | tf_op jit(solution)/shard_map/ppermute | solution.py:25
  33.6 0.7 collective-permute-start.10
  34.3 1.3 %collective-permute-start.8 = (bf16[2,64,512]{2,1,0:T(8,128)(2,1)S(1)}, bf16[2,64,512]{2,1,0:T(8,128)(2,1)S(1)}, u32[]{:S(2)}, u32[]{:S(2)}) collective-permute-start(bf16[2,64,512]{2,1,0:T(8,128)(2,1)S(1)} %collective-permute-done.7), channel_id=1, source_target_pairs={{2,0},{3,1},{10,8},{11,9},{18,16},{19,17},{26,24},{27,25}} | collective-permute-start | bytes 393224 | tf_op jit(solution)/shard_map/ppermute | solution.py:25
  35.7 6.5 %collective-permute-done.8 = bf16[2,64,512]{2,1,0:T(8,128)(2,1)S(1)} collective-permute-done((bf16[2,64,512]{2,1,0:T(8,128)(2,1)S(1)}, bf16[2,64,512]{2,1,0:T(8,128)(2,1)S(1)}, u32[]{:S(2)}, u32[]{:S(2)}) %collective-permute-start.8) | collective-permute-done | bytes 131104 | tf_op jit(solution)/shard_map/ppermute | solution.py:25
  42.2 0.7 collective-permute-start.9
  42.9 3.4 %collective-permute-start.14 = (bf16[2,64,512]{2,1,0:T(8,128)(2,1)S(1)}, bf16[2,64,512]{2,1,0:T(8,128)(2,1)S(1)}, u32[]{:S(2)}, u32[]{:S(2)}) collective-permute-start(bf16[2,64,512]{2,1,0:T(8,128)(2,1)S(1)} %collective-permute-done.7), channel_id=1, source_target_pairs={{0,1},{1,0},{2,3},{3,2},{8,9},{9,8},{10,11},{11,10},{16,17},{17,16... | collective-permute-start | bytes 393224 | tf_op jit(solution)/shard_map/ppermute | solution.py:52
  46.4 2.5 %collective-permute-start.15 = (bf16[2,64,512]{2,1,0:T(8,128)(2,1)S(1)}, bf16[2,64,512]{2,1,0:T(8,128)(2,1)S(1)}, u32[]{:S(2)}, u32[]{:S(2)}) collective-permute-start(bf16[2,64,512]{2,1,0:T(8,128)(2,1)S(1)} %collective-permute-done.8), channel_id=1, source_target_pairs={{0,1},{1,0},{8,9},{9,8},{16,17},{17,16},{24,25},{25,24}} | collective-permute-start | bytes 393224 | tf_op jit(solution)/shard_map/ppermute | solution.py:52
  48.9 1.6 %collective-permute-start = (f32[512,1,128]{2,0,1:T(8,128)S(1)}, f32[512,1,128]{2,0,1:T(8,128)S(1)}, u32[]{:S(2)}, u32[]{:S(2)}) collective-permute-start(f32[512,1,128]{2,0,1:T(8,128)S(1)} %bitcast.112), channel_id=1, source_target_pairs={{0,16},{8,24},{16,0},{24,8},{1,17},{9,25},{17,1},{25,9},{2,18},{10... | collective-permute-start | bytes 786440 | tf_op jit(solution)/shard_map/ppermute | solution.py:72
  51.0 2.2 %collective-permute-done.15 = bf16[2,64,512]{2,1,0:T(8,128)(2,1)S(1)} collective-permute-done((bf16[2,64,512]{2,1,0:T(8,128)(2,1)S(1)}, bf16[2,64,512]{2,1,0:T(8,128)(2,1)S(1)}, u32[]{:S(2)}, u32[]{:S(2)}) %collective-permute-start.15) | collective-permute-done | bytes 131104 | tf_op jit(solution)/shard_map/ppermute | solution.py:52
  53.3 0.7 %fusion.14 = bf16[4,2,2,64,512]{4,3,2,1,0:T(8,128)(2,1)S(1)} fusion(s32[]{:T(128)S(6)} %select_n.83, bf16[4,1,2,64,512]{4,3,2,1,0:T(8,128)(2,1)S(1)} %dynamic-slice_bitcast_fusion.1, bf16[4,1,2,64,512]{4,3,2,1,0:T(8,128)(2,1)S(1)} %dynamic-slice_bitcast_fusion), kind=kLoop, calls=%fused_computation.22 | loop fusion | flops 1572864 | bytes 2097156 | tf_op jit(solution)/shard_map/jit(_roll_dynamic)/concatenate | solution.py:63
  54.1 1.2 %collective-permute-done = f32[512,1,128]{2,0,1:T(8,128)S(1)} collective-permute-done((f32[512,1,128]{2,0,1:T(8,128)S(1)}, f32[512,1,128]{2,0,1:T(8,128)S(1)}, u32[]{:S(2)}, u32[]{:S(2)}) %collective-permute-start) | collective-permute-done | bytes 262176 | tf_op jit(solution)/shard_map/ppermute | solution.py:72
  55.4 1.4 %collective-permute-done.2 = f32[512,1,128]{2,0,1:T(8,128)S(1)} collective-permute-done((f32[512,1,128]{2,0,1:T(8,128)S(1)}, f32[512,1,128]{2,0,1:T(8,128)S(1)}, u32[]{:S(2)}, u32[]{:S(2)}) %collective-permute-start.2) | collective-permute-done | bytes 262176 | tf_op jit(solution)/shard_map/ppermute | solution.py:74
  56.9 3.8 %cosine_convert_fusion = (bf16[2,2,512,1,128]{4,2,0,3,1:T(8,128)(2,1)S(1)}, bf16[2,2,512,1,128]{4,2,0,3,1:T(8,128)(2,1)S(1)}) fusion(f32[2,1,512,1,128]{4,2,0,3,1:T(8,128)S(1)} %maximum_bitcast_fusion.1, f32[2,1,512,1,128]{4,2,0,3,1:T(8,128)S(1)} %maximum_bitcast_fusion, f32[]{:T(128)} %bitcast.4), kind=kLoop, calls=%fused_computation.28 | loop fusion | flops 1310720 | bytes 2097156 | tf_op jit(solution)/shard_map/convert.1
  62.0 1.2 %fusion = f32[1024,512]{1,0:T(8,128)S(1)} fusion(bf16[512,512]{1,0:T(8,128)(2,1)S(1)} %bitcast.115, bf16[512,512]{1,0:T(8,128)(2,1)S(1)} %bitcast.111, bf16[512,512]{1,0:T(8,128)(2,1)S(1)} %bitcast_negate_fusion, bf16[512,512]{1,0:T(8,128)(2,1)S(1)} %get-tuple-element.29, bf16[512,512]{1,0:T(8,128)(2,1)S(1)} %get-tuple-element.30), kind=kOutput, calls=%fused_computation.4 | convolution fusion | flops 1084227584 | bytes 4718592 | tf_op jit(solution)/shard_map/dot_general | solution.py:122
  63.9 1.0 %collective-permute-done.16 = f32[2,1,512]{2,1,0:T(1,128)S(1)} collective-permute-done((f32[2,1,512]{2,1,0:T(1,128)S(1)}, f32[2,1,512]{2,1,0:T(1,128)S(1)}, u32[]{:S(2)}, u32[]{:S(2)}) %collective-permute-start.16) | collective-permute-done | bytes 4128 | tf_op jit(solution)/shard_map/ppermute | solution.py:82
  65.0 1.6 %collective-permute-start.17 = (f32[2,1,512]{2,1,0:T(1,128)S(1)}, f32[2,1,512]{2,1,0:T(1,128)S(1)}, u32[]{:S(2)}, u32[]{:S(2)}) collective-permute-start(f32[2,1,512]{2,1,0:T(1,128)S(1)} %fusion.23), channel_id=1, source_target_pairs={{0,16},{8,24},{16,0},{24,8},{1,17},{9,25},{17,1},{25,9},{2,18},{10... | collective-permute-start | bytes 12296 | tf_op jit(solution)/shard_map/ppermute | solution.py:82
  66.5 2.1 %collective-permute-done.17 = f32[2,1,512]{2,1,0:T(1,128)S(1)} collective-permute-done((f32[2,1,512]{2,1,0:T(1,128)S(1)}, f32[2,1,512]{2,1,0:T(1,128)S(1)}, u32[]{:S(2)}, u32[]{:S(2)}) %collective-permute-start.17) | collective-permute-done | bytes 4128 | tf_op jit(solution)/shard_map/ppermute | solution.py:82
  (54 shorter events, 6.5 us)
Async XLA Ops:
  0.0 35.7 %copy-start = (bf16[1,2,64,512]{3,2,1,0:T(8,128)(2,1)S(1)}, bf16[1,2,64,512]{3,2,1,0:T(8,128)(2,1)}, u32[]{:S(2)}) copy-start(bf16[1,2,64,512]{3,2,1,0:T(8,128)(2,1)} %param.9) | copy-start | bytes 393220
  0.0 21.2 %collective-permute-start.3 = (bf16[2,64,512]{2,1,0:T(8,128)(2,1)}, bf16[2,64,512]{2,1,0:T(8,128)(2,1)S(1)}, u32[]{:S(2)}, u32[]{:S(2)}) collective-permute-start(bf16[2,64,512]{2,1,0:T(8,128)(2,1)} %bitcast.127), channel_id=1, source_target_pairs={{0,2},{1,3},{2,4},{3,5},{4,6},{5,7},{8,10},{9,11},{10,12},{11,13},... | collective-permute-start | bytes 393224 | tf_op jit(solution)/shard_map/ppermute | solution.py:25
  5.1 45.4 %collective-permute-start.12 = (bf16[2,64,512]{2,1,0:T(8,128)(2,1)}, bf16[2,64,512]{2,1,0:T(8,128)(2,1)S(1)}, u32[]{:S(2)}, u32[]{:S(2)}) collective-permute-start(bf16[2,64,512]{2,1,0:T(8,128)(2,1)} %bitcast.128), channel_id=1, source_target_pairs={{0,1},{1,0},{2,3},{3,2},{4,5},{5,4},{6,7},{7,6},{8,9},{9,8},{10,11... | collective-permute-start | bytes 393224 | tf_op jit(solution)/shard_map/ppermute | solution.py:52
  6.7 17.4 %collective-permute-start.6 = (bf16[2,64,512]{2,1,0:T(8,128)(2,1)}, bf16[2,64,512]{2,1,0:T(8,128)(2,1)S(1)}, u32[]{:S(2)}, u32[]{:S(2)}) collective-permute-start(bf16[2,64,512]{2,1,0:T(8,128)(2,1)} %bitcast.129), channel_id=1, source_target_pairs={{2,0},{3,1},{4,2},{5,3},{6,4},{7,5},{10,8},{11,9},{12,10},{13,11},... | collective-permute-start | bytes 393224 | tf_op jit(solution)/shard_map/ppermute | solution.py:25
  15.2 33.6 %all-to-all-start = ((f32[8,64,1,128]{3,1,2,0:T(8,128)}), f32[8,64,1,128]{3,1,2,0:T(8,128)S(1)}, u32[]{:S(2)}, u32[]{:S(2)}) async-start(f32[8,64,1,128]{3,1,2,0:T(8,128)} %constant_dynamic-update-slice_fusion), calls=%async_computation | async-start | bytes 524288 | tf_op jit(solution)/shard_map/all_to_all | solution.py:98
  21.2 4.2 %collective-permute-start.4 = (bf16[2,64,512]{2,1,0:T(8,128)(2,1)S(1)}, bf16[2,64,512]{2,1,0:T(8,128)(2,1)S(1)}, u32[]{:S(2)}, u32[]{:S(2)}) collective-permute-start(bf16[2,64,512]{2,1,0:T(8,128)(2,1)S(1)} %collective-permute-done.3), channel_id=1, source_target_pairs={{2,4},{3,5},{4,6},{5,7},{10,12},{11,13},{12,14},{13,15},{18,20},{1... | collective-permute-start | bytes 393224 | tf_op jit(solution)/shard_map/ppermute | solution.py:25
  24.1 9.6 %collective-permute-start.7 = (bf16[2,64,512]{2,1,0:T(8,128)(2,1)S(1)}, bf16[2,64,512]{2,1,0:T(8,128)(2,1)S(1)}, u32[]{:S(2)}, u32[]{:S(2)}) collective-permute-start(bf16[2,64,512]{2,1,0:T(8,128)(2,1)S(1)} %collective-permute-done.6), channel_id=1, source_target_pairs={{2,0},{3,1},{4,2},{5,3},{10,8},{11,9},{12,10},{13,11},{18,16},{19,... | collective-permute-start | bytes 393224 | tf_op jit(solution)/shard_map/ppermute | solution.py:25
  25.4 8.9 %collective-permute-start.5 = (bf16[2,64,512]{2,1,0:T(8,128)(2,1)S(1)}, bf16[2,64,512]{2,1,0:T(8,128)(2,1)S(1)}, u32[]{:S(2)}, u32[]{:S(2)}) collective-permute-start(bf16[2,64,512]{2,1,0:T(8,128)(2,1)S(1)} %collective-permute-done.4), channel_id=1, source_target_pairs={{4,6},{5,7},{12,14},{13,15},{20,22},{21,23},{28,30},{29,31}} | collective-permute-start | bytes 393224 | tf_op jit(solution)/shard_map/ppermute | solution.py:25
  26.1 22.8 %collective-permute-start.11 = (bf16[2,64,512]{2,1,0:T(8,128)(2,1)S(1)}, bf16[2,64,512]{2,1,0:T(8,128)(2,1)S(1)}, u32[]{:S(2)}, u32[]{:S(2)}) collective-permute-start(bf16[2,64,512]{2,1,0:T(8,128)(2,1)S(1)} %collective-permute-done.3), channel_id=1, source_target_pairs={{2,3},{3,2},{4,5},{5,4},{6,7},{7,6},{10,11},{11,10},{12,13},{13,12... | collective-permute-start | bytes 393224 | tf_op jit(solution)/shard_map/ppermute | solution.py:52
  26.8 23.8 %collective-permute-start.13 = (bf16[2,64,512]{2,1,0:T(8,128)(2,1)S(1)}, bf16[2,64,512]{2,1,0:T(8,128)(2,1)S(1)}, u32[]{:S(2)}, u32[]{:S(2)}) collective-permute-start(bf16[2,64,512]{2,1,0:T(8,128)(2,1)S(1)} %collective-permute-done.6), channel_id=1, source_target_pairs={{0,1},{1,0},{2,3},{3,2},{4,5},{5,4},{8,9},{9,8},{10,11},{11,10},{1... | collective-permute-start | bytes 393224 | tf_op jit(solution)/shard_map/ppermute | solution.py:52
  33.6 12.7 %collective-permute-start.10 = (bf16[2,64,512]{2,1,0:T(8,128)(2,1)S(1)}, bf16[2,64,512]{2,1,0:T(8,128)(2,1)S(1)}, u32[]{:S(2)}, u32[]{:S(2)}) collective-permute-start(bf16[2,64,512]{2,1,0:T(8,128)(2,1)S(1)} %collective-permute-done.4), channel_id=1, source_target_pairs={{4,5},{5,4},{6,7},{7,6},{12,13},{13,12},{14,15},{15,14},{20,21},{2... | collective-permute-start | bytes 393224 | tf_op jit(solution)/shard_map/ppermute | solution.py:52
  34.3 7.9 %collective-permute-start.8 = (bf16[2,64,512]{2,1,0:T(8,128)(2,1)S(1)}, bf16[2,64,512]{2,1,0:T(8,128)(2,1)S(1)}, u32[]{:S(2)}, u32[]{:S(2)}) collective-permute-start(bf16[2,64,512]{2,1,0:T(8,128)(2,1)S(1)} %collective-permute-done.7), channel_id=1, source_target_pairs={{2,0},{3,1},{10,8},{11,9},{18,16},{19,17},{26,24},{27,25}} | collective-permute-start | bytes 393224 | tf_op jit(solution)/shard_map/ppermute | solution.py:25
  42.2 0.7 %collective-permute-start.9 = (bf16[2,64,512]{2,1,0:T(8,128)(2,1)S(1)}, bf16[2,64,512]{2,1,0:T(8,128)(2,1)S(1)}, u32[]{:S(2)}, u32[]{:S(2)}) collective-permute-start(bf16[2,64,512]{2,1,0:T(8,128)(2,1)S(1)} %collective-permute-done.5), channel_id=1, source_target_pairs={{6,7},{7,6},{14,15},{15,14},{22,23},{23,22},{30,31},{31,30}} | collective-permute-start | bytes 393224 | tf_op jit(solution)/shard_map/ppermute | solution.py:52
  42.9 8.1 %collective-permute-start.14 = (bf16[2,64,512]{2,1,0:T(8,128)(2,1)S(1)}, bf16[2,64,512]{2,1,0:T(8,128)(2,1)S(1)}, u32[]{:S(2)}, u32[]{:S(2)}) collective-permute-start(bf16[2,64,512]{2,1,0:T(8,128)(2,1)S(1)} %collective-permute-done.7), channel_id=1, source_target_pairs={{0,1},{1,0},{2,3},{3,2},{8,9},{9,8},{10,11},{11,10},{16,17},{17,16... | collective-permute-start | bytes 393224 | tf_op jit(solution)/shard_map/ppermute | solution.py:52
  46.4 6.9 %collective-permute-start.15 = (bf16[2,64,512]{2,1,0:T(8,128)(2,1)S(1)}, bf16[2,64,512]{2,1,0:T(8,128)(2,1)S(1)}, u32[]{:S(2)}, u32[]{:S(2)}) collective-permute-start(bf16[2,64,512]{2,1,0:T(8,128)(2,1)S(1)} %collective-permute-done.8), channel_id=1, source_target_pairs={{0,1},{1,0},{8,9},{9,8},{16,17},{17,16},{24,25},{25,24}} | collective-permute-start | bytes 393224 | tf_op jit(solution)/shard_map/ppermute | solution.py:52
  48.9 6.4 %collective-permute-start = (f32[512,1,128]{2,0,1:T(8,128)S(1)}, f32[512,1,128]{2,0,1:T(8,128)S(1)}, u32[]{:S(2)}, u32[]{:S(2)}) collective-permute-start(f32[512,1,128]{2,0,1:T(8,128)S(1)} %bitcast.112), channel_id=1, source_target_pairs={{0,16},{8,24},{16,0},{24,8},{1,17},{9,25},{17,1},{25,9},{2,18},{10... | collective-permute-start | bytes 786440 | tf_op jit(solution)/shard_map/ppermute | solution.py:72
  50.5 5.0 %collective-permute-start.1 = (f32[512,1,128]{2,0,1:T(8,128)S(1)}, f32[512,1,128]{2,0,1:T(8,128)S(1)}, u32[]{:S(2)}, u32[]{:S(2)}) collective-permute-start(f32[512,1,128]{2,0,1:T(8,128)S(1)} %bitcast.113), channel_id=1, source_target_pairs={{0,8},{8,0},{16,24},{24,16},{1,9},{9,1},{17,25},{25,17},{2,10},{10... | collective-permute-start | bytes 786440 | tf_op jit(solution)/shard_map/ppermute | solution.py:74
  55.3 1.5 %collective-permute-start.2 = (f32[512,1,128]{2,0,1:T(8,128)S(1)}, f32[512,1,128]{2,0,1:T(8,128)S(1)}, u32[]{:S(2)}, u32[]{:S(2)}) collective-permute-start(f32[512,1,128]{2,0,1:T(8,128)S(1)} %collective-permute-done), channel_id=1, source_target_pairs={{0,8},{8,0},{16,24},{24,16},{1,9},{9,1},{17,25},{25,17},{2,10},{10... | collective-permute-start | bytes 786440 | tf_op jit(solution)/shard_map/ppermute | solution.py:74
  63.7 1.2 %collective-permute-start.16 = (f32[2,1,512]{2,1,0:T(1,128)S(1)}, f32[2,1,512]{2,1,0:T(1,128)S(1)}, u32[]{:S(2)}, u32[]{:S(2)}) collective-permute-start(f32[2,1,512]{2,1,0:T(1,128)S(1)} %pad_maximum_fusion), channel_id=1, source_target_pairs={{0,8},{8,0},{16,24},{24,16},{1,9},{9,1},{17,25},{25,17},{2,10},{10... | collective-permute-start | bytes 12296 | tf_op jit(solution)/shard_map/ppermute | solution.py:82
  65.0 3.7 %collective-permute-start.17 = (f32[2,1,512]{2,1,0:T(1,128)S(1)}, f32[2,1,512]{2,1,0:T(1,128)S(1)}, u32[]{:S(2)}, u32[]{:S(2)}) collective-permute-start(f32[2,1,512]{2,1,0:T(1,128)S(1)} %fusion.23), channel_id=1, source_target_pairs={{0,16},{8,24},{16,0},{24,8},{1,17},{9,25},{17,1},{25,9},{2,18},{10... | collective-permute-start | bytes 12296 | tf_op jit(solution)/shard_map/ppermute | solution.py:82
